TPU v7x, 32 devices: a whole 2x2x4 slice. The times are simulated.
32 devices in a mesh: cell: 8 (over y, x, core), gene: 4 (over z).
Axes of the slice: x: 2, y: 2, z: 4, core: 2. Of those that a mesh axis runs over, the one named last changes fastest.
Arguments:
- expression: float32 [12288, 32768], P('cell', 'gene'), may hold values from -16 to 18, as said below
- tile_mask: int32 [48, 128], P('cell', 'gene'), may hold values from 0 to 1, as said below
- start: float32 [32768, 32], P('gene'), may hold values from -6 to 6
Outputs:
- alphas: float32 [2, 32, 32], replicated
- betas: float32 [2, 32, 32], replicated
- next_block: float32 [32768, 32], P('gene')
Inputs may be any that keep to these rules, and one draw needn't show every extreme that they name: expression: positive mean per gene with gene and cell scales and independent noise. `tile_mask`: each row of tiles belongs to one of 8 cell types and each column of tiles to one of 8 gene modules; a tile is 1 where its type expresses its module.
All inputs are finite; a program needn't handle non-finite values.
Results may differ from a plain program's by a relative error of at most 0.0024.
Values sent between devices are 32-bit elements; how exact they have to be, the bound alone decides.
No kernel may reach another device: no remote copies, remote signals or barrier semaphores. Data moves between devices by JAX's collectives and lax.ppermute only.
A program may use at most 256 MiB of HBM per device.

v0:
```python
import math

import jax
import jax.numpy as jnp
from jax import lax
from jax.experimental import pallas as pl
from jax.experimental.pallas import tpu as pltpu
from jax.sharding import PartitionSpec as P

TILE = 256
STEPS = 2
BF = jnp.bfloat16
F32 = jnp.float32


def split(x):
    p1 = x.astype(BF)
    r1 = x - p1.astype(F32)
    p2 = r1.astype(BF)
    p3 = (r1 - p2.astype(F32)).astype(BF)
    return p1, p2, p3


def butterfly_sum(x, axis):
    n = lax.axis_size(axis)
    if n & (n - 1):
        return lax.psum(x, axis)
    s = 1
    while s < n:
        x = x + lax.ppermute(x, axis, [(i, i ^ s) for i in range(n)])
        s *= 2
    return x


def halving_sum(x, axis, dim):
    n = lax.axis_size(axis)
    if n & (n - 1) or x.shape[dim] % n:
        return lax.psum(x, axis)
    me = lax.axis_index(axis)
    levels = max(n.bit_length() - 2, 0)
    s = 1
    bits = []
    for _ in range(levels):
        half = x.shape[dim] // 2
        bit = (me // s) % 2
        keep = lax.dynamic_slice_in_dim(x, bit * half, half, axis=dim)
        send = lax.dynamic_slice_in_dim(x, (1 - bit) * half, half, axis=dim)
        x = keep + lax.ppermute(send, axis, [(i, i ^ s) for i in range(n)])
        bits.append((s, bit))
        s *= 2
    while s < n:
        x = x + lax.ppermute(x, axis, [(i, i ^ s) for i in range(n)])
        s *= 2
    for s, bit in reversed(bits):
        other = lax.ppermute(x, axis, [(i, i ^ s) for i in range(n)])
        lo_first = jnp.concatenate([x, other], axis=dim)
        hi_first = jnp.concatenate([other, x], axis=dim)
        x = jnp.where(bit == 0, lo_first, hi_first)
    return x


def pack_rows(x, extra):
    w = x.shape[1]
    flat = extra.reshape(-1)
    rows = -(-flat.shape[0] // w)
    flat = jnp.pad(flat, (0, rows * w - flat.shape[0]))
    return jnp.concatenate([x, flat.reshape(rows, w)], axis=0)


def unpack_rows(x, r, extra_shape):
    size = math.prod(extra_shape)
    return x[:r], x[r:].reshape(-1)[:size].reshape(extra_shape)


def gene_sum_with(x, extra):
    r = x.shape[0]
    return unpack_rows(butterfly_sum(pack_rows(x, extra), "gene"), r, extra.shape)


def cell_image_sum(part, extra):
    axis = "cell"
    n = lax.axis_size(axis)
    if n & (n - 1) or part.shape[1] % n:
        return lax.psum(part, axis), lax.psum(extra, axis)
    me = lax.axis_index(axis)
    levels = max(n.bit_length() - 2, 0)
    k = part.shape[0]
    x = part
    s = 1
    bits = []
    for _ in range(levels):
        half = x.shape[1] // 2
        bit = (me // s) % 2
        keep = lax.dynamic_slice_in_dim(x, bit * half, half, axis=1)
        send = lax.dynamic_slice_in_dim(x, (1 - bit) * half, half, axis=1)
        got = lax.ppermute(pack_rows(send, extra), axis, [(i, i ^ s) for i in range(n)])
        got_x, got_e = unpack_rows(got, k, extra.shape)
        x = keep + got_x
        extra = extra + got_e
        bits.append((s, bit))
        s *= 2
    while s < n:
        got = lax.ppermute(pack_rows(x, extra), axis, [(i, i ^ s) for i in range(n)])
        got_x, got_e = unpack_rows(got, k, extra.shape)
        x = x + got_x
        extra = extra + got_e
        s *= 2
    for s, bit in reversed(bits):
        other = lax.ppermute(x, axis, [(i, i ^ s) for i in range(n)])
        lo_first = jnp.concatenate([x, other], axis=1)
        hi_first = jnp.concatenate([other, x], axis=1)
        x = jnp.where(bit == 0, lo_first, hi_first)
    return x, extra


def _nt(a, b):
    return lax.dot_general(a, b, (((1,), (1,)), ((), ())), preferred_element_type=F32)


def _masked(x_ref, m_ref):
    tr, tw = x_ref.shape
    x = x_ref[...].reshape(tr // TILE, TILE, tw) * m_ref[...]
    return x.reshape(tr, tw)


def _pieces(v_ref):
    p = split(v_ref[...])
    return jnp.concatenate(p, axis=0), jnp.concatenate(p[:2], axis=0), p[0]


def forward_kernel(x_ref, m_ref, v_ref, y_ref, *col):
    j = pl.program_id(1)
    k = v_ref.shape[0]
    x = _masked(x_ref, m_ref)
    x1, x2, x3 = split(x)
    s3, s2, s1 = _pieces(v_ref)
    a = _nt(s3, x1)
    c = _nt(s2, x2)
    d = _nt(s1, x3)
    part = ((a[2 * k:] + c[k:] + d) + (a[k:2 * k] + c[:k])) + a[:k]

    @pl.when(j == 0)
    def _():
        y_ref[...] = part

    @pl.when(j > 0)
    def _():
        y_ref[...] += part

    if col:
        (c_ref,) = col
        i = pl.program_id(0)
        tw = x_ref.shape[1]
        s = jnp.sum(x, axis=0, keepdims=True)
        sl = pl.ds(pl.multiple_of(j * tw, tw), tw)

        @pl.when(i == 0)
        def _():
            c_ref[:, sl] = s

        @pl.when(i > 0)
        def _():
            c_ref[:, sl] += s


def backward_kernel(x_ref, m_ref, v_ref, o_ref, *col):
    i = pl.program_id(1)
    k = v_ref.shape[0]
    x = _masked(x_ref, m_ref)
    x1, x2, x3 = split(x)
    p = split(v_ref[...])
    ones = [jnp.ones((8, v_ref.shape[1]), BF)] if col else []
    a = jnp.dot(jnp.concatenate(list(p) + ones, axis=0), x1, preferred_element_type=F32)
    c = jnp.dot(jnp.concatenate(list(p[:2]) + ones, axis=0), x2, preferred_element_type=F32)
    d = jnp.dot(jnp.concatenate(list(p[:1]) + ones, axis=0), x3, preferred_element_type=F32)
    part = ((a[2 * k:3 * k] + c[k:2 * k] + d[:k]) + (a[k:2 * k] + c[:k])) + a[:k]

    @pl.when(i == 0)
    def _():
        o_ref[...] = part

    @pl.when(i > 0)
    def _():
        o_ref[...] += part

    if col:
        (c_ref,) = col
        sums = (d[k:k + 1] + c[2 * k:2 * k + 1]) + a[3 * k:3 * k + 1]

        @pl.when(i == 0)
        def _():
            c_ref[...] = sums

        @pl.when(i > 0)
        def _():
            c_ref[...] += sums


def blocks(rows, width):
    tr = 2 * TILE if rows % (2 * TILE) == 0 else TILE
    tw = min(width, 4096)
    return tr, tw


def forward(expression, mexp, bt, with_colsum):
    rows, width = expression.shape
    k = bt.shape[0]
    tr, tw = blocks(rows, width)
    in_specs = [
        pl.BlockSpec((tr, tw), lambda i, j: (i, j)),
        pl.BlockSpec((tr // TILE, 1, tw), lambda i, j: (i, 0, j)),
        pl.BlockSpec((k, tw), lambda i, j: (0, j)),
    ]
    out_specs = [pl.BlockSpec((k, tr), lambda i, j: (0, i))]
    out_shape = [jax.ShapeDtypeStruct((k, rows), F32)]
    if with_colsum:
        out_specs.append(pl.BlockSpec((1, width), lambda i, j: (0, 0)))
        out_shape.append(jax.ShapeDtypeStruct((1, width), F32))
    return pl.pallas_call(
        forward_kernel,
        grid=(rows // tr, width // tw),
        in_specs=in_specs,
        out_specs=out_specs,
        out_shape=out_shape,
        compiler_params=pltpu.CompilerParams(dimension_semantics=("arbitrary", "arbitrary")),
    )(expression, mexp, bt)


def backward(expression, mexp, yt, with_colsum):
    rows, width = expression.shape
    k = yt.shape[0]
    tr, tw = blocks(rows, width)
    out_specs = [pl.BlockSpec((k, tw), lambda j, i: (0, j))]
    out_shape = [jax.ShapeDtypeStruct((k, width), F32)]
    if with_colsum:
        out_specs.append(pl.BlockSpec((1, tw), lambda j, i: (0, j)))
        out_shape.append(jax.ShapeDtypeStruct((1, width), F32))
    return pl.pallas_call(
        backward_kernel,
        grid=(width // tw, rows // tr),
        in_specs=[
            pl.BlockSpec((tr, tw), lambda j, i: (i, j)),
            pl.BlockSpec((tr // TILE, 1, tw), lambda j, i: (i, 0, j)),
            pl.BlockSpec((k, tr), lambda j, i: (0, i)),
        ],
        out_specs=out_specs,
        out_shape=out_shape,
        compiler_params=pltpu.CompilerParams(dimension_semantics=("arbitrary", "arbitrary")),
    )(expression, mexp, yt)


HI = lax.Precision.HIGHEST


def row_gram(a, b):
    return lax.dot_general(a, b, (((1,), (1,)), ((), ())), precision=HI, preferred_element_type=F32)


def left_solve(lower, x):
    return lax.linalg.triangular_solve(lower, x, left_side=True, lower=True)


def right_solve(lower, x):
    return lax.linalg.triangular_solve(lower, x, left_side=False, lower=True, transpose_a=True)


def per_device(expression, tile_mask, start):
    cell_count = lax.axis_size("cell")
    gene_count = lax.axis_size("gene")
    rows, width = expression.shape
    cells = rows * cell_count
    mexp = jnp.repeat(tile_mask.astype(F32), TILE, axis=1)[:, None, :]
    start_t = jnp.transpose(start)

    y_start = forward(expression, mexp, start_t, False)[0]
    start_t = lax.optimization_barrier((start_t, y_start))[0]
    extra = jnp.concatenate([row_gram(start_t, start_t), jnp.sum(y_start, axis=1)[None, :]], axis=0)
    y_start, extra = gene_sum_with(y_start, extra)
    gram0 = extra[:-1]
    row_total = extra[-1]
    lower0 = jnp.linalg.cholesky(gram0)
    current = left_solve(lower0, start_t)
    y = left_solve(lower0, y_start)

    older = None
    older_side = None
    alpha_list = []
    beta_list = []
    for step in range(STEPS):
        if step > 0:
            y, mean_side = gene_sum_with(forward(expression, mexp, current, False)[0],
                                         jnp.dot(current, means, precision=HI))
        basis = [current] if older is None else [current, older]
        if step == 0:
            part, colsum = backward(expression, mexp, y, True)
            proj_part = jnp.stack([row_gram(v, part) for v in basis])
            ride = jnp.concatenate([proj_part.reshape(-1), colsum[0], row_total])
            raw, ride = cell_image_sum(part, ride)
            proj_cell = ride[:proj_part.size].reshape(proj_part.shape)
            means = ride[proj_part.size:proj_part.size + width] / cells
            mean_side = right_solve(lower0, (ride[proj_part.size + width:] / cells)[None, :])[0]
        else:
            part = backward(expression, mexp, y, False)[0]
            proj_part = jnp.stack([row_gram(v, part) for v in basis])
            raw, proj_cell = cell_image_sum(part, proj_part)
        sides = [mean_side] if older is None else [mean_side, older_side]
        proj_raw = butterfly_sum(proj_cell, "gene")
        image = raw / cells - mean_side[:, None] * means[None, :]
        summed = [proj_raw[t] / cells - sides[t][:, None] * mean_side[None, :] for t in range(len(basis))]
        resid = image - jnp.dot(jnp.transpose(summed[0]), current, precision=HI)
        if older is not None:
            resid = resid - jnp.dot(jnp.transpose(summed[1]), older, precision=HI)
        g = butterfly_sum(row_gram(resid, resid), "gene")
        lower = jnp.linalg.cholesky(g)
        fresh = left_solve(lower, resid)
        alpha_list.append(summed[0])
        beta_list.append(jnp.transpose(lower))
        older = current
        older_side = mean_side
        current = fresh
    next_block = jnp.transpose(current) * math.sqrt(width * gene_count)
    return (jnp.stack(alpha_list), jnp.stack(beta_list), next_block)


def solution(mesh):
    in_specs = (P("cell", "gene"), P("cell", "gene"), P("gene", None))
    out_specs = (P(), P(), P("gene", None))
    return jax.shard_map(
        per_device, mesh=mesh, in_specs=in_specs, out_specs=out_specs, check_vma=False
    )
```

profile of v0, /device:TPU:0, one launch (start us, length us, event | category | flops | bytes accessed | tf_op | source)
XLA Modules:
  0.0 288.4 jit_solution(14450706074146385250)
XLA Ops:
  2.4 27.6 %shard_map.58 = f32[32,1536]{1,0:T(8,128)} custom-call(f32[1536,8192]{1,0:T(8,128)} %x_ref.7, f32[6,1,8192]{2,1,0:T(1,128)} %broadcast_in_dim_reshape.3.m_ref, f32[32,8192]{1,0:T(8,128)} %bitcast.96), custom_call_target="tpu_custom_call" | custom-call | tf_op jit(solution)/shard_map/pallas_call | solution.py:219
  33.3 3.1 %collective-permute-start = (f32[33,1536]{1,0:T(8,128)S(1)}, f32[33,1536]{1,0:T(8,128)S(1)}, u32[]{:S(2)}, u32[]{:S(2)}) collective-permute-start(f32[33,1536]{1,0:T(8,128)S(1)} %pad_maximum_fusion.6), channel_id=1, source_target_pairs={{0,1},{1,0},{2,3},{3,2},{4,5},{5,4},{6,7},{7,6},{8,9},{9,8},{10,11... | collective-permute-start | bytes 608264 | tf_op jit(solution)/shard_map/ppermute | solution.py:30
  36.3 6.0 %collective-permute-done = f32[33,1536]{1,0:T(8,128)S(1)} collective-permute-done((f32[33,1536]{1,0:T(8,128)S(1)}, f32[33,1536]{1,0:T(8,128)S(1)}, u32[]{:S(2)}, u32[]{:S(2)}) %collective-permute-start) | collective-permute-done | bytes 202784 | tf_op jit(solution)/shard_map/ppermute | solution.py:30
  43.3 2.8 collective-permute-start.1
  46.1 10.5 %collective-permute-done.1 = f32[33,1536]{1,0:T(8,128)S(1)} collective-permute-done((f32[33,1536]{1,0:T(8,128)S(1)}, f32[33,1536]{1,0:T(8,128)S(1)}, u32[]{:S(2)}, u32[]{:S(2)}) %collective-permute-start.1) | collective-permute-done | bytes 202784 | tf_op jit(solution)/shard_map/ppermute | solution.py:30
  56.8 2.9 %cholesky.59 = f32[32,32]{1,0:T(8,128)S(1)} custom-call(f32[32,32]{1,0:T(8,128)S(1)} %fusion.24), custom_call_target="Cholesky" | custom-call | tf_op jit(solution)/shard_map/jit(cholesky)/cholesky | solution.py:281
  61.1 2.4 custom-call.13
  65.7 23.4 %shard_map.59 = (f32[32,8192]{1,0:T(8,128)}, f32[1,8192]{1,0:T(1,128)}) custom-call(f32[1536,8192]{1,0:T(8,128)} %x_ref.7, f32[6,1,8192]{2,1,0:T(1,128)} %broadcast_in_dim_reshape.3.m_ref, f32[32,1536]{1,0:T(8,128)} %fusion.7.v_ref), custom_call_target="tpu_custom_call" | custom-call | tf_op jit(solution)/shard_map/pallas_call | solution.py:238
  90.1 2.2 fusion.48
  98.9 8.4 %collective-permute-done.3 = f32[37,2048]{1,0:T(8,128)S(1)} collective-permute-done((f32[37,2048]{1,0:T(8,128)S(1)}, f32[37,2048]{1,0:T(8,128)S(1)}, u32[]{:S(2)}, u32[]{:S(2)}) %collective-permute-start.3) | collective-permute-done | bytes 303136 | tf_op jit(solution)/shard_map/ppermute | solution.py:96
  108.9 7.6 %collective-permute-done.4 = f32[37,2048]{1,0:T(8,128)S(1)} collective-permute-done((f32[37,2048]{1,0:T(8,128)S(1)}, f32[37,2048]{1,0:T(8,128)S(1)}, u32[]{:S(2)}, u32[]{:S(2)}) %collective-permute-start.4) | collective-permute-done | bytes 303136 | tf_op jit(solution)/shard_map/ppermute | solution.py:103
  117.9 5.2 %collective-permute-done.7 = f32[32,2048]{1,0:T(8,128)S(1)} collective-permute-done((f32[32,2048]{1,0:T(8,128)S(1)}, f32[32,2048]{1,0:T(8,128)S(1)}, u32[]{:S(2)}, u32[]{:S(2)}) %collective-permute-start.7) | collective-permute-done | bytes 262176 | tf_op jit(solution)/shard_map/ppermute | solution.py:109
  123.9 3.2 %collective-permute-done.5 = f32[1,32,32]{2,1,0:T(8,128)S(1)} collective-permute-done((f32[1,32,32]{2,1,0:T(8,128)S(1)}, f32[1,32,32]{2,1,0:T(8,128)S(1)}, u32[]{:S(2)}, u32[]{:S(2)}) %collective-permute-start.5) | collective-permute-done | bytes 4128 | tf_op jit(solution)/shard_map/ppermute | solution.py:30
  129.1 2.6 collective-permute-done.6
  134.9 2.8 collective-permute-done.9
  139.7 2.7 collective-permute-done.10
  142.4 2.9 %cholesky.70 = f32[32,32]{1,0:T(8,128)S(1)} custom-call(f32[32,32]{1,0:T(8,128)S(1)} %fusion.18), custom_call_target="Cholesky" | custom-call | tf_op jit(solution)/shard_map/jit(cholesky)/cholesky | solution.py:314
  147.3 2.4 custom-call.14
  151.8 27.6 %shard_map.60 = f32[32,1536]{1,0:T(8,128)} custom-call(f32[1536,8192]{1,0:T(8,128)} %x_ref.7, f32[6,1,8192]{2,1,0:T(1,128)} %broadcast_in_dim_reshape.3.m_ref, f32[32,8192]{1,0:T(8,128)} %fusion.16.v_ref), custom_call_target="tpu_custom_call" | custom-call | tf_op jit(solution)/shard_map/pallas_call | solution.py:219
  182.3 6.8 %collective-permute-done.11 = f32[33,1536]{1,0:T(8,128)S(1)} collective-permute-done((f32[33,1536]{1,0:T(8,128)S(1)}, f32[33,1536]{1,0:T(8,128)S(1)}, u32[]{:S(2)}, u32[]{:S(2)}) %collective-permute-start.11) | collective-permute-done | bytes 202784 | tf_op jit(solution)/shard_map/ppermute | solution.py:30
  191.9 7.2 %collective-permute-done.12 = f32[33,1536]{1,0:T(8,128)S(1)} collective-permute-done((f32[33,1536]{1,0:T(8,128)S(1)}, f32[33,1536]{1,0:T(8,128)S(1)}, u32[]{:S(2)}, u32[]{:S(2)}) %collective-permute-start.12) | collective-permute-done | bytes 202784 | tf_op jit(solution)/shard_map/ppermute | solution.py:30
  199.8 23.1 %shard_map.61 = f32[32,8192]{1,0:T(8,128)} custom-call(f32[1536,8192]{1,0:T(8,128)} %x_ref.7, f32[6,1,8192]{2,1,0:T(1,128)} %broadcast_in_dim_reshape.3.m_ref, f32[32,1536]{1,0:T(8,128)} %slice.146.v_ref), custom_call_target="tpu_custom_call" | custom-call | tf_op jit(solution)/shard_map/pallas_call | solution.py:238
  222.9 2.2 convolution_bitcast_fusion
  225.1 2.2 convolution_bitcast_fusion.1
  235.2 8.2 %collective-permute-done.14 = f32[33,2048]{1,0:T(8,128)S(1)} collective-permute-done((f32[33,2048]{1,0:T(8,128)S(1)}, f32[33,2048]{1,0:T(8,128)S(1)}, u32[]{:S(2)}, u32[]{:S(2)}) %collective-permute-start.14) | collective-permute-done | bytes 270368 | tf_op jit(solution)/shard_map/ppermute | solution.py:96
  245.3 7.2 %collective-permute-done.15 = f32[33,2048]{1,0:T(8,128)S(1)} collective-permute-done((f32[33,2048]{1,0:T(8,128)S(1)}, f32[33,2048]{1,0:T(8,128)S(1)}, u32[]{:S(2)}, u32[]{:S(2)}) %collective-permute-start.15) | collective-permute-done | bytes 270368 | tf_op jit(solution)/shard_map/ppermute | solution.py:103
  255.2 4.1 %collective-permute-done.18 = f32[32,2048]{1,0:T(8,128)S(1)} collective-permute-done((f32[32,2048]{1,0:T(8,128)S(1)}, f32[32,2048]{1,0:T(8,128)S(1)}, u32[]{:S(2)}, u32[]{:S(2)}) %collective-permute-start.18) | collective-permute-done | bytes 262176 | tf_op jit(solution)/shard_map/ppermute | solution.py:109
  260.5 5.2 %collective-permute-done.17 = f32[2,32,32]{2,1,0:T(8,128)S(1)} collective-permute-done((f32[2,32,32]{2,1,0:T(8,128)S(1)}, f32[2,32,32]{2,1,0:T(8,128)S(1)}, u32[]{:S(2)}, u32[]{:S(2)}) %collective-permute-start.17) | collective-permute-done | bytes 8224 | tf_op jit(solution)/shard_map/ppermute | solution.py:30
  270.1 3.4 %collective-permute-done.20 = f32[32,32]{0,1:T(8,128)S(1)} collective-permute-done((f32[32,32]{0,1:T(8,128)S(1)}, f32[32,32]{0,1:T(8,128)S(1)}, u32[]{:S(2)}, u32[]{:S(2)}) %collective-permute-start.20) | collective-permute-done | bytes 4128 | tf_op jit(solution)/shard_map/ppermute | solution.py:30
  275.0 3.1 %collective-permute-done.21 = f32[32,32]{0,1:T(8,128)S(1)} collective-permute-done((f32[32,32]{0,1:T(8,128)S(1)}, f32[32,32]{0,1:T(8,128)S(1)}, u32[]{:S(2)}, u32[]{:S(2)}) %collective-permute-start.21) | collective-permute-done | bytes 4128 | tf_op jit(solution)/shard_map/ppermute | solution.py:30
  278.2 2.9 %cholesky.81 = f32[32,32]{1,0:T(8,128)S(1)} custom-call(f32[32,32]{1,0:T(8,128)S(1)} %fusion.14), custom_call_target="Cholesky" | custom-call | tf_op jit(solution)/shard_map/jit(cholesky)/cholesky | solution.py:314
  282.5 2.4 custom-call.15
  (152 shorter events, 62.6 us)
Async XLA Ops:
  0.6 30.4 %copy-start.1 = (f32[8192,32]{0,1:T(8,128)S(1)}, f32[8192,32]{0,1:T(8,128)}, u32[]{:S(2)}) copy-start(f32[8192,32]{0,1:T(8,128)} %param.8) | copy-start | bytes 3145732
  33.3 9.0 %collective-permute-start = (f32[33,1536]{1,0:T(8,128)S(1)}, f32[33,1536]{1,0:T(8,128)S(1)}, u32[]{:S(2)}, u32[]{:S(2)}) collective-permute-start(f32[33,1536]{1,0:T(8,128)S(1)} %pad_maximum_fusion.6), channel_id=1, source_target_pairs={{0,1},{1,0},{2,3},{3,2},{4,5},{5,4},{6,7},{7,6},{8,9},{9,8},{10,11... | collective-permute-start | bytes 608264 | tf_op jit(solution)/shard_map/ppermute | solution.py:30
  43.3 13.4 %collective-permute-start.1 = (f32[33,1536]{1,0:T(8,128)S(1)}, f32[33,1536]{1,0:T(8,128)S(1)}, u32[]{:S(2)}, u32[]{:S(2)}) collective-permute-start(f32[33,1536]{1,0:T(8,128)S(1)} %fusion.46), channel_id=1, source_target_pairs={{0,2},{1,3},{2,0},{3,1},{4,6},{5,7},{6,4},{7,5},{8,10},{9,11},{10,... | collective-permute-start | bytes 608264 | tf_op jit(solution)/shard_map/ppermute | solution.py:30
  93.3 2.2 collective-permute-start.2
  97.5 9.8 %collective-permute-start.3 = (f32[37,2048]{1,0:T(8,128)S(1)}, f32[37,2048]{1,0:T(8,128)S(1)}, u32[]{:S(2)}, u32[]{:S(2)}) collective-permute-start(f32[37,2048]{1,0:T(8,128)S(1)} %pad_maximum_fusion.2), channel_id=1, source_target_pairs={{0,8},{4,12},{8,0},{12,4},{16,24},{20,28},{24,16},{28,20},{1,9},{5... | collective-permute-start | bytes 909320 | tf_op jit(solution)/shard_map/ppermute | solution.py:96
  107.4 9.0 %collective-permute-start.4 = (f32[37,2048]{1,0:T(8,128)S(1)}, f32[37,2048]{1,0:T(8,128)S(1)}, u32[]{:S(2)}, u32[]{:S(2)}) collective-permute-start(f32[37,2048]{1,0:T(8,128)S(1)} %pad_maximum_fusion.3), channel_id=1, source_target_pairs={{0,16},{4,20},{8,24},{12,28},{16,0},{20,4},{24,8},{28,12},{1,17},{... | collective-permute-start | bytes 909320 | tf_op jit(solution)/shard_map/ppermute | solution.py:103
  116.5 6.7 %collective-permute-start.7 = (f32[32,2048]{1,0:T(8,128)S(1)}, f32[32,2048]{1,0:T(8,128)S(1)}, u32[]{:S(2)}, u32[]{:S(2)}) collective-permute-start(f32[32,2048]{1,0:T(8,128)S(1)} %slice_add_fusion.4), channel_id=1, source_target_pairs={{0,8},{4,12},{8,0},{12,4},{16,24},{20,28},{24,16},{28,20},{1,9},{5... | collective-permute-start | bytes 786440 | tf_op jit(solution)/shard_map/ppermute | solution.py:109
  123.2 8.6 %collective-permute-start.8 = (f32[32,4096]{1,0:T(8,128)S(1)}, f32[32,4096]{1,0:T(8,128)S(1)}, u32[]{:S(2)}, u32[]{:S(2)}) collective-permute-start(f32[32,4096]{1,0:T(8,128)S(1)} %maximum_select_fusion.2), channel_id=1, source_target_pairs={{0,4},{4,0},{8,12},{12,8},{16,20},{20,16},{24,28},{28,24},{1,5},{5... | collective-permute-start | bytes 1572872 | tf_op jit(solution)/shard_map/ppermute | solution.py:109
  123.3 3.7 %collective-permute-start.5 = (f32[1,32,32]{2,1,0:T(8,128)S(1)}, f32[1,32,32]{2,1,0:T(8,128)S(1)}, u32[]{:S(2)}, u32[]{:S(2)}) collective-permute-start(f32[1,32,32]{2,1,0:T(8,128)S(1)} %reshape.197), channel_id=1, source_target_pairs={{0,1},{1,0},{2,3},{3,2},{4,5},{5,4},{6,7},{7,6},{8,9},{9,8},{10,11... | collective-permute-start | bytes 12296 | tf_op jit(solution)/shard_map/ppermute | solution.py:30
  127.1 5.8 %copy-start.3 = (f32[1,32,32]{2,1,0:T(8,128)}, f32[1,32,32]{2,1,0:T(8,128)S(1)}, u32[]{:S(2)}) copy-start(f32[1,32,32]{2,1,0:T(8,128)S(1)} %add.143) | copy-start | bytes 12292
  127.1 4.6 %collective-permute-start.6 = (f32[1,32,32]{2,1,0:T(8,128)S(1)}, f32[1,32,32]{2,1,0:T(8,128)S(1)}, u32[]{:S(2)}, u32[]{:S(2)}) collective-permute-start(f32[1,32,32]{2,1,0:T(8,128)S(1)} %add.143), channel_id=1, source_target_pairs={{0,2},{1,3},{2,0},{3,1},{4,6},{5,7},{6,4},{7,5},{8,10},{9,11},{10,... | collective-permute-start | bytes 12296 | tf_op jit(solution)/shard_map/ppermute | solution.py:30
  129.1 13.3 %copy-start.7 = (f32[32]{0:T(128)}, f32[32]{0:T(128)S(1)}, u32[]{:S(2)}) copy-start(f32[32]{0:T(128)S(1)} %convolution_bitcast_fusion.3) | copy-start | bytes 388
  131.7 7.9 %copy-start.6 = (f32[1,32,32]{2,1,0:T(8,128)}, f32[1,32,32]{2,1,0:T(8,128)S(1)}, u32[]{:S(2)}) copy-start(f32[1,32,32]{2,1,0:T(8,128)S(1)} %collective-permute-done.6) | copy-start | bytes 12292
  133.9 3.8 %collective-permute-start.9 = (f32[32,32]{0,1:T(8,128)S(1)}, f32[32,32]{0,1:T(8,128)S(1)}, u32[]{:S(2)}, u32[]{:S(2)}) collective-permute-start(f32[32,32]{0,1:T(8,128)S(1)} %fusion.49), channel_id=1, source_target_pairs={{0,1},{1,0},{2,3},{3,2},{4,5},{5,4},{6,7},{7,6},{8,9},{9,8},{10,11... | collective-permute-start | bytes 12296 | tf_op jit(solution)/shard_map/ppermute | solution.py:30
  137.7 4.6 %collective-permute-start.10 = (f32[32,32]{0,1:T(8,128)S(1)}, f32[32,32]{0,1:T(8,128)S(1)}, u32[]{:S(2)}, u32[]{:S(2)}) collective-permute-start(f32[32,32]{0,1:T(8,128)S(1)} %add.146), channel_id=1, source_target_pairs={{0,2},{1,3},{2,0},{3,1},{4,6},{5,7},{6,4},{7,5},{8,10},{9,11},{10,... | collective-permute-start | bytes 12296 | tf_op jit(solution)/shard_map/ppermute | solution.py:30
  151.8 27.6 %copy-start = (f32[32,8192]{1,0:T(8,128)S(1)}, f32[32,8192]{1,0:T(8,128)}, u32[]{:S(2)}) copy-start(f32[32,8192]{1,0:T(8,128)} %fusion.16.v_ref) | copy-start | bytes 3145732
  181.3 7.8 %collective-permute-start.11 = (f32[33,1536]{1,0:T(8,128)S(1)}, f32[33,1536]{1,0:T(8,128)S(1)}, u32[]{:S(2)}, u32[]{:S(2)}) collective-permute-start(f32[33,1536]{1,0:T(8,128)S(1)} %pad_maximum_fusion.7), channel_id=1, source_target_pairs={{0,1},{1,0},{2,3},{3,2},{4,5},{5,4},{6,7},{7,6},{8,9},{9,8},{10,11... | collective-permute-start | bytes 608264 | tf_op jit(solution)/shard_map/ppermute | solution.py:30
  190.1 9.0 %collective-permute-start.12 = (f32[33,1536]{1,0:T(8,128)S(1)}, f32[33,1536]{1,0:T(8,128)S(1)}, u32[]{:S(2)}, u32[]{:S(2)}) collective-permute-start(f32[33,1536]{1,0:T(8,128)S(1)} %fusion.45), channel_id=1, source_target_pairs={{0,2},{1,3},{2,0},{3,1},{4,6},{5,7},{6,4},{7,5},{8,10},{9,11},{10,... | collective-permute-start | bytes 608264 | tf_op jit(solution)/shard_map/ppermute | solution.py:30
  225.1 3.3 %copy-start.4 = (f32[1,32,32]{2,1,0:T(8,128)}, f32[1,32,32]{2,1,0:T(8,128)S(1)}, u32[]{:S(2)}) copy-start(f32[1,32,32]{2,1,0:T(8,128)S(1)} %convolution_bitcast_fusion) | copy-start | bytes 12292
  227.3 1.1 copy-start.5
  228.5 0.6 copy-start.2
  229.2 2.3 collective-permute-start.13
  233.6 9.8 %collective-permute-start.14 = (f32[33,2048]{1,0:T(8,128)S(1)}, f32[33,2048]{1,0:T(8,128)S(1)}, u32[]{:S(2)}, u32[]{:S(2)}) collective-permute-start(f32[33,2048]{1,0:T(8,128)S(1)} %pad_maximum_fusion.4), channel_id=1, source_target_pairs={{0,8},{4,12},{8,0},{12,4},{16,24},{20,28},{24,16},{28,20},{1,9},{5... | collective-permute-start | bytes 811016 | tf_op jit(solution)/shard_map/ppermute | solution.py:96
  243.6 9.0 %collective-permute-start.15 = (f32[33,2048]{1,0:T(8,128)S(1)}, f32[33,2048]{1,0:T(8,128)S(1)}, u32[]{:S(2)}, u32[]{:S(2)}) collective-permute-start(f32[33,2048]{1,0:T(8,128)S(1)} %pad_maximum_fusion.5), channel_id=1, source_target_pairs={{0,16},{4,20},{8,24},{12,28},{16,0},{20,4},{24,8},{28,12},{1,17},{... | collective-permute-start | bytes 811016 | tf_op jit(solution)/shard_map/ppermute | solution.py:103
  252.6 6.7 %collective-permute-start.18 = (f32[32,2048]{1,0:T(8,128)S(1)}, f32[32,2048]{1,0:T(8,128)S(1)}, u32[]{:S(2)}, u32[]{:S(2)}) collective-permute-start(f32[32,2048]{1,0:T(8,128)S(1)} %slice_add_fusion.2), channel_id=1, source_target_pairs={{0,8},{4,12},{8,0},{12,4},{16,24},{20,28},{24,16},{28,20},{1,9},{5... | collective-permute-start | bytes 786440 | tf_op jit(solution)/shard_map/ppermute | solution.py:109
  255.0 5.2 %collective-permute-start.16 = (f32[2,32,32]{2,1,0:T(8,128)S(1)}, f32[2,32,32]{2,1,0:T(8,128)S(1)}, u32[]{:S(2)}, u32[]{:S(2)}) collective-permute-start(f32[2,32,32]{2,1,0:T(8,128)S(1)} %add_add_fusion), channel_id=1, source_target_pairs={{0,1},{1,0},{2,3},{3,2},{4,5},{5,4},{6,7},{7,6},{8,9},{9,8},{10,11... | collective-permute-start | bytes 24584 | tf_op jit(solution)/shard_map/ppermute | solution.py:30
  259.3 7.5 %collective-permute-start.19 = (f32[32,4096]{1,0:T(8,128)S(1)}, f32[32,4096]{1,0:T(8,128)S(1)}, u32[]{:S(2)}, u32[]{:S(2)}) collective-permute-start(f32[32,4096]{1,0:T(8,128)S(1)} %maximum_select_fusion.3), channel_id=1, source_target_pairs={{0,4},{4,0},{8,12},{12,8},{16,20},{20,16},{24,28},{28,24},{1,5},{5... | collective-permute-start | bytes 1572872 | tf_op jit(solution)/shard_map/ppermute | solution.py:109
  260.2 5.5 %collective-permute-start.17 = (f32[2,32,32]{2,1,0:T(8,128)S(1)}, f32[2,32,32]{2,1,0:T(8,128)S(1)}, u32[]{:S(2)}, u32[]{:S(2)}) collective-permute-start(f32[2,32,32]{2,1,0:T(8,128)S(1)} %add.157), channel_id=1, source_target_pairs={{0,2},{1,3},{2,0},{3,1},{4,6},{5,7},{6,4},{7,5},{8,10},{9,11},{10,... | collective-permute-start | bytes 24584 | tf_op jit(solution)/shard_map/ppermute | solution.py:30
  269.7 3.8 %collective-permute-start.20 = (f32[32,32]{0,1:T(8,128)S(1)}, f32[32,32]{0,1:T(8,128)S(1)}, u32[]{:S(2)}, u32[]{:S(2)}) collective-permute-start(f32[32,32]{0,1:T(8,128)S(1)} %fusion.50), channel_id=1, source_target_pairs={{0,1},{1,0},{2,3},{3,2},{4,5},{5,4},{6,7},{7,6},{8,9},{9,8},{10,11... | collective-permute-start | bytes 12296 | tf_op jit(solution)/shard_map/ppermute | solution.py:30
  273.5 4.6 %collective-permute-start.21 = (f32[32,32]{0,1:T(8,128)S(1)}, f32[32,32]{0,1:T(8,128)S(1)}, u32[]{:S(2)}, u32[]{:S(2)}) collective-permute-start(f32[32,32]{0,1:T(8,128)S(1)} %add.160), channel_id=1, source_target_pairs={{0,2},{1,3},{2,0},{3,1},{4,6},{5,7},{6,4},{7,5},{8,10},{9,11},{10,... | collective-permute-start | bytes 12296 | tf_op jit(solution)/shard_map/ppermute | solution.py:30
where the time goes:
time: 289 us; the launch traced here: 288 us
  Pallas kernels  102 us (35%)
  waiting for transfers between devices  97.8 us (34%)
  other arithmetic  34.7 us (12%)
  starting transfers between devices  25 us (9%)
  matrix products  20.9 us (7%)
  local copies, waits for them, and re-layouts  7.17 us (2%)
    pallas_call x2, Pallas kernels, forward(): pl.pallas_call(forward_kernel, grid=(rows // tr, width // tw), in_specs=i...  55.2 us
    ppermute x12, waiting for transfers between devices, butterfly_sum(): x = x + lax.ppermute(x, axis, [(i, i ^ s) for i in range(n)])  53.6 us
    pallas_call x2, Pallas kernels, backward(): pl.pallas_call(backward_kernel, grid=(width // tw, rows // tr), in_specs=...  46.5 us
    ppermute x4, waiting for transfers between devices, cell_image_sum(): lax.ppermute(pack_rows(send, extra), axis, [(i, i ^ s) for i in range(n)])  20.1 us
    ppermute x12, starting transfers between devices, butterfly_sum(): x = x + lax.ppermute(x, axis, [(i, i ^ s) for i in range(n)])  15.7 us
    ppermute x2, waiting for transfers between devices, cell_image_sum(): lax.ppermute(pack_rows(x, extra), axis, [(i, i ^ s) for i in range(n)])  14.8 us
    dot_general x6, matrix products, row_gram(): lax.dot_general(a, b, (((1,), (1,)), ((), ())), precision=HI, preferred_e...  9.46 us
    ppermute x4, waiting for transfers between devices, cell_image_sum(): other = lax.ppermute(x, axis, [(i, i ^ s) for i in range(n)])  9.3 us
  transfers between devices with their start and end apart: 22, of which 19 were waited for; matrix products, arithmetic and copies ran while one was open for 2% of the time, Pallas kernels for 0%

commit v1 on v0

--- a/solution.py
+++ b/solution.py
@@ -288,8 +288,10 @@
     beta_list = []
     for step in range(STEPS):
         if step > 0:
-            y, mean_side = gene_sum_with(forward(expression, mexp, current, False)[0],
-                                         jnp.dot(current, means, precision=HI))
+            y, side = gene_sum_with(forward(expression, mexp, last_resid, False)[0],
+                                    jnp.dot(last_resid, means, precision=HI))
+            y = left_solve(last_lower, y)
+            mean_side = left_solve(last_lower, side[:, None])[:, 0]
         basis = [current] if older is None else [current, older]
         if step == 0:
             part, colsum = backward(expression, mexp, y, True)
@@ -318,6 +320,8 @@
         older = current
         older_side = mean_side
         current = fresh
+        last_resid = resid
+        last_lower = lower
     next_block = jnp.transpose(current) * math.sqrt(width * gene_count)
     return (jnp.stack(alpha_list), jnp.stack(beta_list), next_block)
 

time: 289 us -> 279 us (0.965)
  waiting for transfers between devices: 97.8 us -> 83.9 us
    ppermute x12, waiting for transfers between devices: 53.6 us -> 40.1 us  [butterfly_sum(): x = x + lax.ppermute(x, axis, [(i, i ^ s) for i in range(n)])]
    another operation x4 -> x6, matrix products: 6.18 us -> 8.29 us  [left_solve(): return lax.linalg.triangular_solve(lower, x, left_side=True, lower=True)]
  transfers between devices with their start and end apart: 22 -> 22, of which waited for: 19 -> 17; matrix products, arithmetic and copies ran while one was open for 2% -> 6% of each run, Pallas kernels for 0% -> 10%
where the time goes in v1:
time: 279 us; the launch traced here: 278 us
  Pallas kernels  102 us (37%)
  waiting for transfers between devices  83.9 us (30%)
  other arithmetic  34.7 us (12%)
  starting transfers between devices  26.1 us (9%)
  matrix products  23 us (8%)
  local copies, waits for them, and re-layouts  7.07 us (3%)
    pallas_call x2, Pallas kernels, forward(): pl.pallas_call(forward_kernel, grid=(rows // tr, width // tw), in_specs=i...  55.1 us
    pallas_call x2, Pallas kernels, backward(): pl.pallas_call(backward_kernel, grid=(width // tw, rows // tr), in_specs=...  46.5 us
    ppermute x12, waiting for transfers between devices, butterfly_sum(): x = x + lax.ppermute(x, axis, [(i, i ^ s) for i in range(n)])  40.1 us
    ppermute x4, waiting for transfers between devices, cell_image_sum(): lax.ppermute(pack_rows(send, extra), axis, [(i, i ^ s) for i in range(n)])  19.9 us
    ppermute x12, starting transfers between devices, butterfly_sum(): x = x + lax.ppermute(x, axis, [(i, i ^ s) for i in range(n)])  16.4 us
    ppermute x2, waiting for transfers between devices, cell_image_sum(): lax.ppermute(pack_rows(x, extra), axis, [(i, i ^ s) for i in range(n)])  14.7 us
    dot_general x6, matrix products, row_gram(): lax.dot_general(a, b, (((1,), (1,)), ((), ())), precision=HI, preferred_e...  9.45 us
    ppermute x4, waiting for transfers between devices, cell_image_sum(): other = lax.ppermute(x, axis, [(i, i ^ s) for i in range(n)])  9.25 us
  transfers between devices with their start and end apart: 22, of which 17 were waited for; matrix products, arithmetic and copies ran while one was open for 6% of the time, Pallas kernels for 10%

profile of v1, /device:TPU:0, one launch (start us, length us, event | category | flops | bytes accessed | tf_op | source)
XLA Modules:
  0.0 277.6 jit_solution(10078257710181700632)
XLA Ops:
  2.4 27.6 %shard_map.58 = f32[32,1536]{1,0:T(8,128)} custom-call(f32[1536,8192]{1,0:T(8,128)} %x_ref.7, f32[6,1,8192]{2,1,0:T(1,128)} %broadcast_in_dim_reshape.3.m_ref, f32[32,8192]{1,0:T(8,128)} %bitcast.110), custom_call_target="tpu_custom_call" | custom-call | tf_op jit(solution)/shard_map/pallas_call | solution.py:219
  33.3 3.1 %collective-permute-start = (f32[33,1536]{1,0:T(8,128)S(1)}, f32[33,1536]{1,0:T(8,128)S(1)}, u32[]{:S(2)}, u32[]{:S(2)}) collective-permute-start(f32[33,1536]{1,0:T(8,128)S(1)} %pad_maximum_fusion.6), channel_id=1, source_target_pairs={{0,1},{1,0},{2,3},{3,2},{4,5},{5,4},{6,7},{7,6},{8,9},{9,8},{10,11... | collective-permute-start | bytes 608264 | tf_op jit(solution)/shard_map/ppermute | solution.py:30
  36.4 6.0 %collective-permute-done = f32[33,1536]{1,0:T(8,128)S(1)} collective-permute-done((f32[33,1536]{1,0:T(8,128)S(1)}, f32[33,1536]{1,0:T(8,128)S(1)}, u32[]{:S(2)}, u32[]{:S(2)}) %collective-permute-start) | collective-permute-done | bytes 202784 | tf_op jit(solution)/shard_map/ppermute | solution.py:30
  43.3 2.8 %collective-permute-start.1 = (f32[33,1536]{1,0:T(8,128)S(1)}, f32[33,1536]{1,0:T(8,128)S(1)}, u32[]{:S(2)}, u32[]{:S(2)}) collective-permute-start(f32[33,1536]{1,0:T(8,128)S(1)} %fusion.50), channel_id=1, source_target_pairs={{0,2},{1,3},{2,0},{3,1},{4,6},{5,7},{6,4},{7,5},{8,10},{9,11},{10,... | collective-permute-start | bytes 608264 | tf_op jit(solution)/shard_map/ppermute | solution.py:30
  46.1 10.6 %collective-permute-done.1 = f32[33,1536]{1,0:T(8,128)S(1)} collective-permute-done((f32[33,1536]{1,0:T(8,128)S(1)}, f32[33,1536]{1,0:T(8,128)S(1)}, u32[]{:S(2)}, u32[]{:S(2)}) %collective-permute-start.1) | collective-permute-done | bytes 202784 | tf_op jit(solution)/shard_map/ppermute | solution.py:30
  56.9 2.9 %cholesky.59 = f32[32,32]{1,0:T(8,128)S(1)} custom-call(f32[32,32]{1,0:T(8,128)S(1)} %fusion.28), custom_call_target="Cholesky" | custom-call | tf_op jit(solution)/shard_map/jit(cholesky)/cholesky | solution.py:281
  61.1 2.4 custom-call.19
  65.7 23.4 %shard_map.59 = (f32[32,8192]{1,0:T(8,128)}, f32[1,8192]{1,0:T(1,128)}) custom-call(f32[1536,8192]{1,0:T(8,128)} %x_ref.7, f32[6,1,8192]{2,1,0:T(1,128)} %broadcast_in_dim_reshape.3.m_ref, f32[32,1536]{1,0:T(8,128)} %fusion.9.v_ref), custom_call_target="tpu_custom_call" | custom-call | tf_op jit(solution)/shard_map/pallas_call | solution.py:238
  90.2 2.2 fusion.52
  98.9 8.4 %collective-permute-done.3 = f32[37,2048]{1,0:T(8,128)S(1)} collective-permute-done((f32[37,2048]{1,0:T(8,128)S(1)}, f32[37,2048]{1,0:T(8,128)S(1)}, u32[]{:S(2)}, u32[]{:S(2)}) %collective-permute-start.3) | collective-permute-done | bytes 303136 | tf_op jit(solution)/shard_map/ppermute | solution.py:96
  108.9 7.6 %collective-permute-done.4 = f32[37,2048]{1,0:T(8,128)S(1)} collective-permute-done((f32[37,2048]{1,0:T(8,128)S(1)}, f32[37,2048]{1,0:T(8,128)S(1)}, u32[]{:S(2)}, u32[]{:S(2)}) %collective-permute-start.4) | collective-permute-done | bytes 303136 | tf_op jit(solution)/shard_map/ppermute | solution.py:103
  117.9 5.2 %collective-permute-done.7 = f32[32,2048]{1,0:T(8,128)S(1)} collective-permute-done((f32[32,2048]{1,0:T(8,128)S(1)}, f32[32,2048]{1,0:T(8,128)S(1)}, u32[]{:S(2)}, u32[]{:S(2)}) %collective-permute-start.7) | collective-permute-done | bytes 262176 | tf_op jit(solution)/shard_map/ppermute | solution.py:109
  123.9 3.2 %collective-permute-done.5 = f32[1,32,32]{2,1,0:T(8,128)S(1)} collective-permute-done((f32[1,32,32]{2,1,0:T(8,128)S(1)}, f32[1,32,32]{2,1,0:T(8,128)S(1)}, u32[]{:S(2)}, u32[]{:S(2)}) %collective-permute-start.5) | collective-permute-done | bytes 4128 | tf_op jit(solution)/shard_map/ppermute | solution.py:30
  129.1 2.6 collective-permute-done.6
  136.0 27.6 %shard_map.60 = f32[32,1536]{1,0:T(8,128)} custom-call(f32[1536,8192]{1,0:T(8,128)} %x_ref.7, f32[6,1,8192]{2,1,0:T(1,128)} %broadcast_in_dim_reshape.3.m_ref, f32[32,8192]{1,0:T(8,128)} %copy-done), custom_call_target="tpu_custom_call" | custom-call | tf_op jit(solution)/shard_map/pallas_call | solution.py:219
  163.6 3.0 %collective-permute-start.10 = (f32[32,32]{0,1:T(8,128)S(1)}, f32[32,32]{0,1:T(8,128)S(1)}, u32[]{:S(2)}, u32[]{:S(2)}) collective-permute-start(f32[32,32]{0,1:T(8,128)S(1)} %add.147), channel_id=1, source_target_pairs={{0,2},{1,3},{2,0},{3,1},{4,6},{5,7},{6,4},{7,5},{8,10},{9,11},{10,... | collective-permute-start | bytes 12296 | tf_op jit(solution)/shard_map/ppermute | solution.py:30
  168.5 2.9 %cholesky.70 = f32[32,32]{1,0:T(8,128)S(1)} custom-call(f32[32,32]{1,0:T(8,128)S(1)} %fusion.22), custom_call_target="Cholesky" | custom-call | tf_op jit(solution)/shard_map/jit(cholesky)/cholesky | solution.py:316
  173.3 2.4 custom-call.21
  176.8 3.1 %collective-permute-start.12 = (f32[33,1536]{1,0:T(8,128)S(1)}, f32[33,1536]{1,0:T(8,128)S(1)}, u32[]{:S(2)}, u32[]{:S(2)}) collective-permute-start(f32[33,1536]{1,0:T(8,128)S(1)} %fusion.49), channel_id=1, source_target_pairs={{0,2},{1,3},{2,0},{3,1},{4,6},{5,7},{6,4},{7,5},{8,10},{9,11},{10,... | collective-permute-start | bytes 608264 | tf_op jit(solution)/shard_map/ppermute | solution.py:30
  179.9 2.2 fusion.20
  182.1 5.6 %collective-permute-done.12 = f32[33,1536]{1,0:T(8,128)S(1)} collective-permute-done((f32[33,1536]{1,0:T(8,128)S(1)}, f32[33,1536]{1,0:T(8,128)S(1)}, u32[]{:S(2)}, u32[]{:S(2)}) %collective-permute-start.12) | collective-permute-done | bytes 202784 | tf_op jit(solution)/shard_map/ppermute | solution.py:30
  188.9 23.1 %shard_map.61 = f32[32,8192]{1,0:T(8,128)} custom-call(f32[1536,8192]{1,0:T(8,128)} %x_ref.7, f32[6,1,8192]{2,1,0:T(1,128)} %broadcast_in_dim_reshape.3.m_ref, f32[32,1536]{1,0:T(8,128)} %fusion.7.v_ref), custom_call_target="tpu_custom_call" | custom-call | tf_op jit(solution)/shard_map/pallas_call | solution.py:238
  212.0 2.2 convolution_bitcast_fusion
  215.2 2.2 convolution_bitcast_fusion.1
  225.0 8.1 %collective-permute-done.14 = f32[33,2048]{1,0:T(8,128)S(1)} collective-permute-done((f32[33,2048]{1,0:T(8,128)S(1)}, f32[33,2048]{1,0:T(8,128)S(1)}, u32[]{:S(2)}, u32[]{:S(2)}) %collective-permute-start.14) | collective-permute-done | bytes 270368 | tf_op jit(solution)/shard_map/ppermute | solution.py:96
  235.0 7.1 %collective-permute-done.15 = f32[33,2048]{1,0:T(8,128)S(1)} collective-permute-done((f32[33,2048]{1,0:T(8,128)S(1)}, f32[33,2048]{1,0:T(8,128)S(1)}, u32[]{:S(2)}, u32[]{:S(2)}) %collective-permute-start.15) | collective-permute-done | bytes 270368 | tf_op jit(solution)/shard_map/ppermute | solution.py:103
  244.8 4.0 %collective-permute-done.18 = f32[32,2048]{1,0:T(8,128)S(1)} collective-permute-done((f32[32,2048]{1,0:T(8,128)S(1)}, f32[32,2048]{1,0:T(8,128)S(1)}, u32[]{:S(2)}, u32[]{:S(2)}) %collective-permute-start.18) | collective-permute-done | bytes 262176 | tf_op jit(solution)/shard_map/ppermute | solution.py:109
  250.7 4.2 %collective-permute-done.17 = f32[2,32,32]{2,1,0:T(8,128)S(1)} collective-permute-done((f32[2,32,32]{2,1,0:T(8,128)S(1)}, f32[2,32,32]{2,1,0:T(8,128)S(1)}, u32[]{:S(2)}, u32[]{:S(2)}) %collective-permute-start.17) | collective-permute-done | bytes 8224 | tf_op jit(solution)/shard_map/ppermute | solution.py:30
  259.1 3.7 %collective-permute-done.20 = f32[32,32]{0,1:T(8,128)S(1)} collective-permute-done((f32[32,32]{0,1:T(8,128)S(1)}, f32[32,32]{0,1:T(8,128)S(1)}, u32[]{:S(2)}, u32[]{:S(2)}) %collective-permute-start.20) | collective-permute-done | bytes 4128 | tf_op jit(solution)/shard_map/ppermute | solution.py:30
  264.0 3.4 %collective-permute-done.21 = f32[32,32]{0,1:T(8,128)S(1)} collective-permute-done((f32[32,32]{0,1:T(8,128)S(1)}, f32[32,32]{0,1:T(8,128)S(1)}, u32[]{:S(2)}, u32[]{:S(2)}) %collective-permute-start.21) | collective-permute-done | bytes 4128 | tf_op jit(solution)/shard_map/ppermute | solution.py:30
  267.5 2.9 %cholesky.81 = f32[32,32]{1,0:T(8,128)S(1)} custom-call(f32[32,32]{1,0:T(8,128)S(1)} %fusion.16), custom_call_target="Cholesky" | custom-call | tf_op jit(solution)/shard_map/jit(cholesky)/cholesky | solution.py:316
  271.8 2.4 custom-call.23
  (154 shorter events, 58.2 us)
Async XLA Ops:
  0.6 30.5 %copy-start.1 = (f32[8192,32]{0,1:T(8,128)S(1)}, f32[8192,32]{0,1:T(8,128)}, u32[]{:S(2)}) copy-start(f32[8192,32]{0,1:T(8,128)} %param.10) | copy-start | bytes 3145732
  33.3 9.0 %collective-permute-start = (f32[33,1536]{1,0:T(8,128)S(1)}, f32[33,1536]{1,0:T(8,128)S(1)}, u32[]{:S(2)}, u32[]{:S(2)}) collective-permute-start(f32[33,1536]{1,0:T(8,128)S(1)} %pad_maximum_fusion.6), channel_id=1, source_target_pairs={{0,1},{1,0},{2,3},{3,2},{4,5},{5,4},{6,7},{7,6},{8,9},{9,8},{10,11... | collective-permute-start | bytes 608264 | tf_op jit(solution)/shard_map/ppermute | solution.py:30
  43.3 13.4 %collective-permute-start.1 = (f32[33,1536]{1,0:T(8,128)S(1)}, f32[33,1536]{1,0:T(8,128)S(1)}, u32[]{:S(2)}, u32[]{:S(2)}) collective-permute-start(f32[33,1536]{1,0:T(8,128)S(1)} %fusion.50), channel_id=1, source_target_pairs={{0,2},{1,3},{2,0},{3,1},{4,6},{5,7},{6,4},{7,5},{8,10},{9,11},{10,... | collective-permute-start | bytes 608264 | tf_op jit(solution)/shard_map/ppermute | solution.py:30
  93.3 2.2 collective-permute-start.2
  97.5 9.8 %collective-permute-start.3 = (f32[37,2048]{1,0:T(8,128)S(1)}, f32[37,2048]{1,0:T(8,128)S(1)}, u32[]{:S(2)}, u32[]{:S(2)}) collective-permute-start(f32[37,2048]{1,0:T(8,128)S(1)} %pad_maximum_fusion.2), channel_id=1, source_target_pairs={{0,8},{4,12},{8,0},{12,4},{16,24},{20,28},{24,16},{28,20},{1,9},{5... | collective-permute-start | bytes 909320 | tf_op jit(solution)/shard_map/ppermute | solution.py:96
  107.4 9.0 %collective-permute-start.4 = (f32[37,2048]{1,0:T(8,128)S(1)}, f32[37,2048]{1,0:T(8,128)S(1)}, u32[]{:S(2)}, u32[]{:S(2)}) collective-permute-start(f32[37,2048]{1,0:T(8,128)S(1)} %pad_maximum_fusion.3), channel_id=1, source_target_pairs={{0,16},{4,20},{8,24},{12,28},{16,0},{20,4},{24,8},{28,12},{1,17},{... | collective-permute-start | bytes 909320 | tf_op jit(solution)/shard_map/ppermute | solution.py:103
  116.5 6.7 %collective-permute-start.7 = (f32[32,2048]{1,0:T(8,128)S(1)}, f32[32,2048]{1,0:T(8,128)S(1)}, u32[]{:S(2)}, u32[]{:S(2)}) collective-permute-start(f32[32,2048]{1,0:T(8,128)S(1)} %slice_add_fusion.4), channel_id=1, source_target_pairs={{0,8},{4,12},{8,0},{12,4},{16,24},{20,28},{24,16},{28,20},{1,9},{5... | collective-permute-start | bytes 786440 | tf_op jit(solution)/shard_map/ppermute | solution.py:109
  123.2 8.6 %collective-permute-start.8 = (f32[32,4096]{1,0:T(8,128)S(1)}, f32[32,4096]{1,0:T(8,128)S(1)}, u32[]{:S(2)}, u32[]{:S(2)}) collective-permute-start(f32[32,4096]{1,0:T(8,128)S(1)} %maximum_select_fusion.2), channel_id=1, source_target_pairs={{0,4},{4,0},{8,12},{12,8},{16,20},{20,16},{24,28},{28,24},{1,5},{5... | collective-permute-start | bytes 1572872 | tf_op jit(solution)/shard_map/ppermute | solution.py:109
  123.4 3.7 %collective-permute-start.5 = (f32[1,32,32]{2,1,0:T(8,128)S(1)}, f32[1,32,32]{2,1,0:T(8,128)S(1)}, u32[]{:S(2)}, u32[]{:S(2)}) collective-permute-start(f32[1,32,32]{2,1,0:T(8,128)S(1)} %reshape.200), channel_id=1, source_target_pairs={{0,1},{1,0},{2,3},{3,2},{4,5},{5,4},{6,7},{7,6},{8,9},{9,8},{10,11... | collective-permute-start | bytes 12296 | tf_op jit(solution)/shard_map/ppermute | solution.py:30
  127.1 5.9 %copy-start.3 = (f32[1,32,32]{2,1,0:T(8,128)}, f32[1,32,32]{2,1,0:T(8,128)S(1)}, u32[]{:S(2)}) copy-start(f32[1,32,32]{2,1,0:T(8,128)S(1)} %add.144) | copy-start | bytes 12292
  127.1 4.6 %collective-permute-start.6 = (f32[1,32,32]{2,1,0:T(8,128)S(1)}, f32[1,32,32]{2,1,0:T(8,128)S(1)}, u32[]{:S(2)}, u32[]{:S(2)}) collective-permute-start(f32[1,32,32]{2,1,0:T(8,128)S(1)} %add.144), channel_id=1, source_target_pairs={{0,2},{1,3},{2,0},{3,1},{4,6},{5,7},{6,4},{7,5},{8,10},{9,11},{10,... | collective-permute-start | bytes 12296 | tf_op jit(solution)/shard_map/ppermute | solution.py:30
  129.1 2.6 copy-start.8
  131.7 2.2 copy-start.7
  133.0 3.0 %copy-start = (f32[32,8192]{1,0:T(8,128)}, f32[32,8192]{1,0:T(8,128)S(1)}, u32[]{:S(2)}) copy-start(f32[32,8192]{1,0:T(8,128)S(1)} %fusion.3.v_ref) | copy-start | bytes 3145732
  134.0 29.6 %collective-permute-start.9 = (f32[32,32]{0,1:T(8,128)S(1)}, f32[32,32]{0,1:T(8,128)S(1)}, u32[]{:S(2)}, u32[]{:S(2)}) collective-permute-start(f32[32,32]{0,1:T(8,128)S(1)} %fusion.53), channel_id=1, source_target_pairs={{0,1},{1,0},{2,3},{3,2},{4,5},{5,4},{6,7},{7,6},{8,9},{9,8},{10,11... | collective-permute-start | bytes 12296 | tf_op jit(solution)/shard_map/ppermute | solution.py:30
  163.6 4.8 %collective-permute-start.10 = (f32[32,32]{0,1:T(8,128)S(1)}, f32[32,32]{0,1:T(8,128)S(1)}, u32[]{:S(2)}, u32[]{:S(2)}) collective-permute-start(f32[32,32]{0,1:T(8,128)S(1)} %add.147), channel_id=1, source_target_pairs={{0,2},{1,3},{2,0},{3,1},{4,6},{5,7},{6,4},{7,5},{8,10},{9,11},{10,... | collective-permute-start | bytes 12296 | tf_op jit(solution)/shard_map/ppermute | solution.py:30
  167.5 8.3 %collective-permute-start.11 = (f32[33,1536]{1,0:T(8,128)S(1)}, f32[33,1536]{1,0:T(8,128)S(1)}, u32[]{:S(2)}, u32[]{:S(2)}) collective-permute-start(f32[33,1536]{1,0:T(8,128)S(1)} %pad_maximum_fusion.7), channel_id=1, source_target_pairs={{0,1},{1,0},{2,3},{3,2},{4,5},{5,4},{6,7},{7,6},{8,9},{9,8},{10,11... | collective-permute-start | bytes 608264 | tf_op jit(solution)/shard_map/ppermute | solution.py:30
  175.8 36.2 %copy-start.4 = (f32[1,32,32]{1,2,0:T(8,128)}, f32[1,32,32]{1,2,0:T(8,128)S(1)}, u32[]{:S(2)}) copy-start(f32[1,32,32]{1,2,0:T(8,128)S(1)} %custom-call.21) | copy-start | bytes 12292
  176.8 11.0 %collective-permute-start.12 = (f32[33,1536]{1,0:T(8,128)S(1)}, f32[33,1536]{1,0:T(8,128)S(1)}, u32[]{:S(2)}, u32[]{:S(2)}) collective-permute-start(f32[33,1536]{1,0:T(8,128)S(1)} %fusion.49), channel_id=1, source_target_pairs={{0,2},{1,3},{2,0},{3,1},{4,6},{5,7},{6,4},{7,5},{8,10},{9,11},{10,... | collective-permute-start | bytes 608264 | tf_op jit(solution)/shard_map/ppermute | solution.py:30
  214.1 3.3 %copy-start.5 = (f32[1,32,32]{2,1,0:T(8,128)}, f32[1,32,32]{2,1,0:T(8,128)S(1)}, u32[]{:S(2)}) copy-start(f32[1,32,32]{2,1,0:T(8,128)S(1)} %convolution_bitcast_fusion) | copy-start | bytes 12292
  217.5 0.6 copy-start.6
  218.1 0.6 copy-start.2
  218.7 2.3 collective-permute-start.13
  223.2 9.8 %collective-permute-start.14 = (f32[33,2048]{1,0:T(8,128)S(1)}, f32[33,2048]{1,0:T(8,128)S(1)}, u32[]{:S(2)}, u32[]{:S(2)}) collective-permute-start(f32[33,2048]{1,0:T(8,128)S(1)} %pad_maximum_fusion.4), channel_id=1, source_target_pairs={{0,8},{4,12},{8,0},{12,4},{16,24},{20,28},{24,16},{28,20},{1,9},{5... | collective-permute-start | bytes 811016 | tf_op jit(solution)/shard_map/ppermute | solution.py:96
  233.1 9.0 %collective-permute-start.15 = (f32[33,2048]{1,0:T(8,128)S(1)}, f32[33,2048]{1,0:T(8,128)S(1)}, u32[]{:S(2)}, u32[]{:S(2)}) collective-permute-start(f32[33,2048]{1,0:T(8,128)S(1)} %pad_maximum_fusion.5), channel_id=1, source_target_pairs={{0,16},{4,20},{8,24},{12,28},{16,0},{20,4},{24,8},{28,12},{1,17},{... | collective-permute-start | bytes 811016 | tf_op jit(solution)/shard_map/ppermute | solution.py:103
  242.2 6.7 %collective-permute-start.18 = (f32[32,2048]{1,0:T(8,128)S(1)}, f32[32,2048]{1,0:T(8,128)S(1)}, u32[]{:S(2)}, u32[]{:S(2)}) collective-permute-start(f32[32,2048]{1,0:T(8,128)S(1)} %slice_add_fusion.2), channel_id=1, source_target_pairs={{0,8},{4,12},{8,0},{12,4},{16,24},{20,28},{24,16},{28,20},{1,9},{5... | collective-permute-start | bytes 786440 | tf_op jit(solution)/shard_map/ppermute | solution.py:109
  244.7 5.0 %collective-permute-start.16 = (f32[2,32,32]{2,1,0:T(8,128)S(1)}, f32[2,32,32]{2,1,0:T(8,128)S(1)}, u32[]{:S(2)}, u32[]{:S(2)}) collective-permute-start(f32[2,32,32]{2,1,0:T(8,128)S(1)} %add_add_fusion), channel_id=1, source_target_pairs={{0,1},{1,0},{2,3},{3,2},{4,5},{5,4},{6,7},{7,6},{8,9},{9,8},{10,11... | collective-permute-start | bytes 24584 | tf_op jit(solution)/shard_map/ppermute | solution.py:30
  248.9 7.2 %collective-permute-start.19 = (f32[32,4096]{1,0:T(8,128)S(1)}, f32[32,4096]{1,0:T(8,128)S(1)}, u32[]{:S(2)}, u32[]{:S(2)}) collective-permute-start(f32[32,4096]{1,0:T(8,128)S(1)} %maximum_select_fusion.3), channel_id=1, source_target_pairs={{0,4},{4,0},{8,12},{12,8},{16,20},{20,16},{24,28},{28,24},{1,5},{5... | collective-permute-start | bytes 1572872 | tf_op jit(solution)/shard_map/ppermute | solution.py:109
  249.8 5.2 %collective-permute-start.17 = (f32[2,32,32]{2,1,0:T(8,128)S(1)}, f32[2,32,32]{2,1,0:T(8,128)S(1)}, u32[]{:S(2)}, u32[]{:S(2)}) collective-permute-start(f32[2,32,32]{2,1,0:T(8,128)S(1)} %add.158), channel_id=1, source_target_pairs={{0,2},{1,3},{2,0},{3,1},{4,6},{5,7},{6,4},{7,5},{8,10},{9,11},{10,... | collective-permute-start | bytes 24584 | tf_op jit(solution)/shard_map/ppermute | solution.py:30
  259.0 3.8 %collective-permute-start.20 = (f32[32,32]{0,1:T(8,128)S(1)}, f32[32,32]{0,1:T(8,128)S(1)}, u32[]{:S(2)}, u32[]{:S(2)}) collective-permute-start(f32[32,32]{0,1:T(8,128)S(1)} %fusion.54), channel_id=1, source_target_pairs={{0,1},{1,0},{2,3},{3,2},{4,5},{5,4},{6,7},{7,6},{8,9},{9,8},{10,11... | collective-permute-start | bytes 12296 | tf_op jit(solution)/shard_map/ppermute | solution.py:30
  262.8 4.6 %collective-permute-start.21 = (f32[32,32]{0,1:T(8,128)S(1)}, f32[32,32]{0,1:T(8,128)S(1)}, u32[]{:S(2)}, u32[]{:S(2)}) collective-permute-start(f32[32,32]{0,1:T(8,128)S(1)} %add.161), channel_id=1, source_target_pairs={{0,2},{1,3},{2,0},{3,1},{4,6},{5,7},{6,4},{7,5},{8,10},{9,11},{10,... | collective-permute-start | bytes 12296 | tf_op jit(solution)/shard_map/ppermute | solution.py:30

commit v2 on v1

--- a/solution.py
+++ b/solution.py
@@ -280,7 +280,7 @@
     row_total = extra[-1]
     lower0 = jnp.linalg.cholesky(gram0)
     current = left_solve(lower0, start_t)
-    y = left_solve(lower0, y_start)
+    y = y_start
 
     older = None
     older_side = None
@@ -298,7 +298,8 @@
             proj_part = jnp.stack([row_gram(v, part) for v in basis])
             ride = jnp.concatenate([proj_part.reshape(-1), colsum[0], row_total])
             raw, ride = cell_image_sum(part, ride)
-            proj_cell = ride[:proj_part.size].reshape(proj_part.shape)
+            raw = left_solve(lower0, raw)
+            proj_cell = right_solve(lower0, ride[:proj_part.size].reshape(proj_part.shape)[0])[None]
             means = ride[proj_part.size:proj_part.size + width] / cells
             mean_side = right_solve(lower0, (ride[proj_part.size + width:] / cells)[None, :])[0]
         else:

time: 279 us -> 278 us (level)
  transfers between devices with their start and end apart: 22 -> 22, of which waited for: 17 -> 17; matrix products, arithmetic and copies ran while one was open for 6% -> 7% of each run, Pallas kernels for 10% -> 10%
where the time goes in v2:
time: 278 us; the launch traced here: 277 us
  Pallas kernels  102 us (37%)
  waiting for transfers between devices  82.5 us (30%)
  other arithmetic  34.7 us (12%)
  starting transfers between devices  26.1 us (9%)
  matrix products  23.1 us (8%)
  local copies, waits for them, and re-layouts  8.13 us (3%)
    pallas_call x2, Pallas kernels, forward(): pl.pallas_call(forward_kernel, grid=(rows // tr, width // tw), in_specs=i...  55.1 us
    pallas_call x2, Pallas kernels, backward(): pl.pallas_call(backward_kernel, grid=(width // tw, rows // tr), in_specs=...  46.5 us
    ppermute x12, waiting for transfers between devices, butterfly_sum(): x = x + lax.ppermute(x, axis, [(i, i ^ s) for i in range(n)])  39 us
    ppermute x4, waiting for transfers between devices, cell_image_sum(): lax.ppermute(pack_rows(send, extra), axis, [(i, i ^ s) for i in range(n)])  19.9 us
    ppermute x12, starting transfers between devices, butterfly_sum(): x = x + lax.ppermute(x, axis, [(i, i ^ s) for i in range(n)])  16.4 us
    ppermute x2, waiting for transfers between devices, cell_image_sum(): lax.ppermute(pack_rows(x, extra), axis, [(i, i ^ s) for i in range(n)])  14.7 us
    dot_general x6, matrix products, row_gram(): lax.dot_general(a, b, (((1,), (1,)), ((), ())), precision=HI, preferred_e...  9.45 us
    ppermute x4, waiting for transfers between devices, cell_image_sum(): other = lax.ppermute(x, axis, [(i, i ^ s) for i in range(n)])  8.88 us
  transfers between devices with their start and end apart: 22, of which 17 were waited for; matrix products, arithmetic and copies ran while one was open for 7% of the time, Pallas kernels for 10%

profile of v2, /device:TPU:0, one launch (start us, length us, event | category | flops | bytes accessed | tf_op | source)
XLA Modules:
  0.0 277.3 jit_solution(12225355088132862275)
XLA Ops:
  2.4 27.6 %shard_map.58 = f32[32,1536]{1,0:T(8,128)} custom-call(f32[1536,8192]{1,0:T(8,128)} %x_ref.7, f32[6,1,8192]{2,1,0:T(1,128)} %broadcast_in_dim_reshape.3.m_ref, f32[32,8192]{1,0:T(8,128)} %bitcast.110), custom_call_target="tpu_custom_call" | custom-call | tf_op jit(solution)/shard_map/pallas_call | solution.py:219
  33.3 3.1 %collective-permute-start = (f32[33,1536]{1,0:T(8,128)S(1)}, f32[33,1536]{1,0:T(8,128)S(1)}, u32[]{:S(2)}, u32[]{:S(2)}) collective-permute-start(f32[33,1536]{1,0:T(8,128)S(1)} %pad_maximum_fusion.6), channel_id=1, source_target_pairs={{0,1},{1,0},{2,3},{3,2},{4,5},{5,4},{6,7},{7,6},{8,9},{9,8},{10,11... | collective-permute-start | bytes 608264 | tf_op jit(solution)/shard_map/ppermute | solution.py:30
  36.4 6.0 %collective-permute-done = f32[33,1536]{1,0:T(8,128)S(1)} collective-permute-done((f32[33,1536]{1,0:T(8,128)S(1)}, f32[33,1536]{1,0:T(8,128)S(1)}, u32[]{:S(2)}, u32[]{:S(2)}) %collective-permute-start) | collective-permute-done | bytes 202784 | tf_op jit(solution)/shard_map/ppermute | solution.py:30
  43.3 2.8 %collective-permute-start.1 = (f32[33,1536]{1,0:T(8,128)S(1)}, f32[33,1536]{1,0:T(8,128)S(1)}, u32[]{:S(2)}, u32[]{:S(2)}) collective-permute-start(f32[33,1536]{1,0:T(8,128)S(1)} %fusion.54), channel_id=1, source_target_pairs={{0,2},{1,3},{2,0},{3,1},{4,6},{5,7},{6,4},{7,5},{8,10},{9,11},{10,... | collective-permute-start | bytes 608264 | tf_op jit(solution)/shard_map/ppermute | solution.py:30
  46.1 10.6 %collective-permute-done.1 = f32[33,1536]{1,0:T(8,128)S(1)} collective-permute-done((f32[33,1536]{1,0:T(8,128)S(1)}, f32[33,1536]{1,0:T(8,128)S(1)}, u32[]{:S(2)}, u32[]{:S(2)}) %collective-permute-start.1) | collective-permute-done | bytes 202784 | tf_op jit(solution)/shard_map/ppermute | solution.py:30
  57.6 2.9 %cholesky.59 = f32[32,32]{1,0:T(8,128)S(1)} custom-call(f32[32,32]{1,0:T(8,128)S(1)} %fusion.31), custom_call_target="Cholesky" | custom-call | tf_op jit(solution)/shard_map/jit(cholesky)/cholesky | solution.py:281
  61.8 2.4 custom-call.20
  64.2 23.4 %shard_map.59 = (f32[32,8192]{1,0:T(8,128)}, f32[1,8192]{1,0:T(1,128)}) custom-call(f32[1536,8192]{1,0:T(8,128)} %x_ref.7, f32[6,1,8192]{2,1,0:T(1,128)} %broadcast_in_dim_reshape.3.m_ref, f32[32,1536]{1,0:T(8,128)} %slice.160.v_ref), custom_call_target="tpu_custom_call" | custom-call | tf_op jit(solution)/shard_map/pallas_call | solution.py:238
  89.8 2.2 fusion.56
  93.0 2.0 collective-permute-done.2
  98.5 8.4 %collective-permute-done.3 = f32[37,2048]{1,0:T(8,128)S(1)} collective-permute-done((f32[37,2048]{1,0:T(8,128)S(1)}, f32[37,2048]{1,0:T(8,128)S(1)}, u32[]{:S(2)}, u32[]{:S(2)}) %collective-permute-start.3) | collective-permute-done | bytes 303136 | tf_op jit(solution)/shard_map/ppermute | solution.py:96
  108.5 7.6 %collective-permute-done.4 = f32[37,2048]{1,0:T(8,128)S(1)} collective-permute-done((f32[37,2048]{1,0:T(8,128)S(1)}, f32[37,2048]{1,0:T(8,128)S(1)}, u32[]{:S(2)}, u32[]{:S(2)}) %collective-permute-start.4) | collective-permute-done | bytes 303136 | tf_op jit(solution)/shard_map/ppermute | solution.py:103
  117.9 4.9 %collective-permute-done.7 = f32[32,2048]{1,0:T(8,128)S(1)} collective-permute-done((f32[32,2048]{1,0:T(8,128)S(1)}, f32[32,2048]{1,0:T(8,128)S(1)}, u32[]{:S(2)}, u32[]{:S(2)}) %collective-permute-start.7) | collective-permute-done | bytes 262176 | tf_op jit(solution)/shard_map/ppermute | solution.py:109
  123.8 3.1 %collective-permute-done.5 = f32[1,32,32]{2,1,0:T(8,128)S(1)} collective-permute-done((f32[1,32,32]{2,1,0:T(8,128)S(1)}, f32[1,32,32]{2,1,0:T(8,128)S(1)}, u32[]{:S(2)}, u32[]{:S(2)}) %collective-permute-start.5) | collective-permute-done | bytes 4128 | tf_op jit(solution)/shard_map/ppermute | solution.py:30
  135.6 27.6 %shard_map.60 = f32[32,1536]{1,0:T(8,128)} custom-call(f32[1536,8192]{1,0:T(8,128)} %x_ref.7, f32[6,1,8192]{2,1,0:T(1,128)} %broadcast_in_dim_reshape.3.m_ref, f32[32,8192]{1,0:T(8,128)} %copy-done), custom_call_target="tpu_custom_call" | custom-call | tf_op jit(solution)/shard_map/pallas_call | solution.py:219
  163.3 3.0 %collective-permute-start.10 = (f32[32,32]{0,1:T(8,128)S(1)}, f32[32,32]{0,1:T(8,128)S(1)}, u32[]{:S(2)}, u32[]{:S(2)}) collective-permute-start(f32[32,32]{0,1:T(8,128)S(1)} %add.162), channel_id=1, source_target_pairs={{0,2},{1,3},{2,0},{3,1},{4,6},{5,7},{6,4},{7,5},{8,10},{9,11},{10,... | collective-permute-start | bytes 12296 | tf_op jit(solution)/shard_map/ppermute | solution.py:30
  168.2 2.9 %cholesky.70 = f32[32,32]{1,0:T(8,128)S(1)} custom-call(f32[32,32]{1,0:T(8,128)S(1)} %fusion.25), custom_call_target="Cholesky" | custom-call | tf_op jit(solution)/shard_map/jit(cholesky)/cholesky | solution.py:317
  173.0 2.4 custom-call.22
  176.4 3.1 %collective-permute-start.12 = (f32[33,1536]{1,0:T(8,128)S(1)}, f32[33,1536]{1,0:T(8,128)S(1)}, u32[]{:S(2)}, u32[]{:S(2)}) collective-permute-start(f32[33,1536]{1,0:T(8,128)S(1)} %fusion.53), channel_id=1, source_target_pairs={{0,2},{1,3},{2,0},{3,1},{4,6},{5,7},{6,4},{7,5},{8,10},{9,11},{10,... | collective-permute-start | bytes 608264 | tf_op jit(solution)/shard_map/ppermute | solution.py:30
  179.6 2.2 fusion.23
  181.8 5.7 %collective-permute-done.12 = f32[33,1536]{1,0:T(8,128)S(1)} collective-permute-done((f32[33,1536]{1,0:T(8,128)S(1)}, f32[33,1536]{1,0:T(8,128)S(1)}, u32[]{:S(2)}, u32[]{:S(2)}) %collective-permute-start.12) | collective-permute-done | bytes 202784 | tf_op jit(solution)/shard_map/ppermute | solution.py:30
  188.6 23.1 %shard_map.61 = f32[32,8192]{1,0:T(8,128)} custom-call(f32[1536,8192]{1,0:T(8,128)} %x_ref.7, f32[6,1,8192]{2,1,0:T(1,128)} %broadcast_in_dim_reshape.3.m_ref, f32[32,1536]{1,0:T(8,128)} %fusion.11.v_ref), custom_call_target="tpu_custom_call" | custom-call | tf_op jit(solution)/shard_map/pallas_call | solution.py:238
  211.7 2.2 convolution_bitcast_fusion
  214.9 2.2 convolution_bitcast_fusion.1
  224.7 8.1 %collective-permute-done.14 = f32[33,2048]{1,0:T(8,128)S(1)} collective-permute-done((f32[33,2048]{1,0:T(8,128)S(1)}, f32[33,2048]{1,0:T(8,128)S(1)}, u32[]{:S(2)}, u32[]{:S(2)}) %collective-permute-start.14) | collective-permute-done | bytes 270368 | tf_op jit(solution)/shard_map/ppermute | solution.py:96
  234.7 7.1 %collective-permute-done.15 = f32[33,2048]{1,0:T(8,128)S(1)} collective-permute-done((f32[33,2048]{1,0:T(8,128)S(1)}, f32[33,2048]{1,0:T(8,128)S(1)}, u32[]{:S(2)}, u32[]{:S(2)}) %collective-permute-start.15) | collective-permute-done | bytes 270368 | tf_op jit(solution)/shard_map/ppermute | solution.py:103
  244.5 4.0 %collective-permute-done.18 = f32[32,2048]{1,0:T(8,128)S(1)} collective-permute-done((f32[32,2048]{1,0:T(8,128)S(1)}, f32[32,2048]{1,0:T(8,128)S(1)}, u32[]{:S(2)}, u32[]{:S(2)}) %collective-permute-start.18) | collective-permute-done | bytes 262176 | tf_op jit(solution)/shard_map/ppermute | solution.py:109
  250.4 4.2 %collective-permute-done.17 = f32[2,32,32]{2,1,0:T(8,128)S(1)} collective-permute-done((f32[2,32,32]{2,1,0:T(8,128)S(1)}, f32[2,32,32]{2,1,0:T(8,128)S(1)}, u32[]{:S(2)}, u32[]{:S(2)}) %collective-permute-start.17) | collective-permute-done | bytes 8224 | tf_op jit(solution)/shard_map/ppermute | solution.py:30
  258.8 3.7 %collective-permute-done.20 = f32[32,32]{0,1:T(8,128)S(1)} collective-permute-done((f32[32,32]{0,1:T(8,128)S(1)}, f32[32,32]{0,1:T(8,128)S(1)}, u32[]{:S(2)}, u32[]{:S(2)}) %collective-permute-start.20) | collective-permute-done | bytes 4128 | tf_op jit(solution)/shard_map/ppermute | solution.py:30
  263.7 3.4 %collective-permute-done.21 = f32[32,32]{0,1:T(8,128)S(1)} collective-permute-done((f32[32,32]{0,1:T(8,128)S(1)}, f32[32,32]{0,1:T(8,128)S(1)}, u32[]{:S(2)}, u32[]{:S(2)}) %collective-permute-start.21) | collective-permute-done | bytes 4128 | tf_op jit(solution)/shard_map/ppermute | solution.py:30
  267.2 2.9 %cholesky.81 = f32[32,32]{1,0:T(8,128)S(1)} custom-call(f32[32,32]{1,0:T(8,128)S(1)} %fusion.19), custom_call_target="Cholesky" | custom-call | tf_op jit(solution)/shard_map/jit(cholesky)/cholesky | solution.py:317
  271.5 2.4 custom-call.23
  (161 shorter events, 58.9 us)
Async XLA Ops:
  0.6 30.5 %copy-start.1 = (f32[8192,32]{0,1:T(8,128)S(1)}, f32[8192,32]{0,1:T(8,128)}, u32[]{:S(2)}) copy-start(f32[8192,32]{0,1:T(8,128)} %param.8) | copy-start | bytes 3145732
  33.3 9.0 %collective-permute-start = (f32[33,1536]{1,0:T(8,128)S(1)}, f32[33,1536]{1,0:T(8,128)S(1)}, u32[]{:S(2)}, u32[]{:S(2)}) collective-permute-start(f32[33,1536]{1,0:T(8,128)S(1)} %pad_maximum_fusion.6), channel_id=1, source_target_pairs={{0,1},{1,0},{2,3},{3,2},{4,5},{5,4},{6,7},{7,6},{8,9},{9,8},{10,11... | collective-permute-start | bytes 608264 | tf_op jit(solution)/shard_map/ppermute | solution.py:30
  43.3 13.4 %collective-permute-start.1 = (f32[33,1536]{1,0:T(8,128)S(1)}, f32[33,1536]{1,0:T(8,128)S(1)}, u32[]{:S(2)}, u32[]{:S(2)}) collective-permute-start(f32[33,1536]{1,0:T(8,128)S(1)} %fusion.54), channel_id=1, source_target_pairs={{0,2},{1,3},{2,0},{3,1},{4,6},{5,7},{6,4},{7,5},{8,10},{9,11},{10,... | collective-permute-start | bytes 608264 | tf_op jit(solution)/shard_map/ppermute | solution.py:30
  92.9 2.2 collective-permute-start.2
  97.1 9.8 %collective-permute-start.3 = (f32[37,2048]{1,0:T(8,128)S(1)}, f32[37,2048]{1,0:T(8,128)S(1)}, u32[]{:S(2)}, u32[]{:S(2)}) collective-permute-start(f32[37,2048]{1,0:T(8,128)S(1)} %pad_maximum_fusion.2), channel_id=1, source_target_pairs={{0,8},{4,12},{8,0},{12,4},{16,24},{20,28},{24,16},{28,20},{1,9},{5... | collective-permute-start | bytes 909320 | tf_op jit(solution)/shard_map/ppermute | solution.py:96
  107.1 9.0 %collective-permute-start.4 = (f32[37,2048]{1,0:T(8,128)S(1)}, f32[37,2048]{1,0:T(8,128)S(1)}, u32[]{:S(2)}, u32[]{:S(2)}) collective-permute-start(f32[37,2048]{1,0:T(8,128)S(1)} %pad_maximum_fusion.3), channel_id=1, source_target_pairs={{0,16},{4,20},{8,24},{12,28},{16,0},{20,4},{24,8},{28,12},{1,17},{... | collective-permute-start | bytes 909320 | tf_op jit(solution)/shard_map/ppermute | solution.py:103
  116.1 6.7 %collective-permute-start.7 = (f32[32,2048]{1,0:T(8,128)S(1)}, f32[32,2048]{1,0:T(8,128)S(1)}, u32[]{:S(2)}, u32[]{:S(2)}) collective-permute-start(f32[32,2048]{1,0:T(8,128)S(1)} %slice_add_fusion.4), channel_id=1, source_target_pairs={{0,8},{4,12},{8,0},{12,4},{16,24},{20,28},{24,16},{28,20},{1,9},{5... | collective-permute-start | bytes 786440 | tf_op jit(solution)/shard_map/ppermute | solution.py:109
  122.8 6.0 %collective-permute-start.8 = (f32[32,4096]{1,0:T(8,128)S(1)}, f32[32,4096]{1,0:T(8,128)S(1)}, u32[]{:S(2)}, u32[]{:S(2)}) collective-permute-start(f32[32,4096]{1,0:T(8,128)S(1)} %maximum_select_fusion.3), channel_id=1, source_target_pairs={{0,4},{4,0},{8,12},{12,8},{16,20},{20,16},{24,28},{28,24},{1,5},{5... | collective-permute-start | bytes 1572872 | tf_op jit(solution)/shard_map/ppermute | solution.py:109
  123.2 3.8 %collective-permute-start.5 = (f32[1,32,32]{2,1,0:T(8,128)S(1)}, f32[1,32,32]{2,1,0:T(8,128)S(1)}, u32[]{:S(2)}, u32[]{:S(2)}) collective-permute-start(f32[1,32,32]{2,1,0:T(8,128)S(1)} %convolution_bitcast_fusion.2), channel_id=1, source_target_pairs={{0,1},{1,0},{2,3},{3,2},{4,5},{5,4},{6,7},{7,6},{8,9},{9,8},{10,11... | collective-permute-start | bytes 12296 | tf_op jit(solution)/shard_map/ppermute | solution.py:30
  123.8 7.7 %copy-start.8 = (f32[32]{0:T(128)}, f32[32]{0:T(128)S(1)}, u32[]{:S(2)}) copy-start(f32[32]{0:T(128)S(1)} %convolution_bitcast_fusion.5) | copy-start | bytes 388
  126.9 5.8 %copy-start.3 = (f32[1,32,32]{2,1,0:T(8,128)}, f32[1,32,32]{2,1,0:T(8,128)S(1)}, u32[]{:S(2)}) copy-start(f32[1,32,32]{2,1,0:T(8,128)S(1)} %add.158) | copy-start | bytes 12292
  126.9 4.6 %collective-permute-start.6 = (f32[1,32,32]{2,1,0:T(8,128)S(1)}, f32[1,32,32]{2,1,0:T(8,128)S(1)}, u32[]{:S(2)}, u32[]{:S(2)}) collective-permute-start(f32[1,32,32]{2,1,0:T(8,128)S(1)} %add.158), channel_id=1, source_target_pairs={{0,2},{1,3},{2,0},{3,1},{4,6},{5,7},{6,4},{7,5},{8,10},{9,11},{10,... | collective-permute-start | bytes 12296 | tf_op jit(solution)/shard_map/ppermute | solution.py:30
  131.6 50.2 %copy-start.7 = (f32[1,32,32]{2,1,0:T(8,128)}, f32[1,32,32]{2,1,0:T(8,128)S(1)}, u32[]{:S(2)}) copy-start(f32[1,32,32]{2,1,0:T(8,128)S(1)} %collective-permute-done.6) | copy-start | bytes 12292
  132.7 2.9 %copy-start = (f32[32,8192]{1,0:T(8,128)}, f32[32,8192]{1,0:T(8,128)S(1)}, u32[]{:S(2)}) copy-start(f32[32,8192]{1,0:T(8,128)S(1)} %convolution_subtract_fusion.1.v_ref) | copy-start | bytes 3145732
  133.7 29.6 %collective-permute-start.9 = (f32[32,32]{0,1:T(8,128)S(1)}, f32[32,32]{0,1:T(8,128)S(1)}, u32[]{:S(2)}, u32[]{:S(2)}) collective-permute-start(f32[32,32]{0,1:T(8,128)S(1)} %fusion.57), channel_id=1, source_target_pairs={{0,1},{1,0},{2,3},{3,2},{4,5},{5,4},{6,7},{7,6},{8,9},{9,8},{10,11... | collective-permute-start | bytes 12296 | tf_op jit(solution)/shard_map/ppermute | solution.py:30
  163.3 4.8 %collective-permute-start.10 = (f32[32,32]{0,1:T(8,128)S(1)}, f32[32,32]{0,1:T(8,128)S(1)}, u32[]{:S(2)}, u32[]{:S(2)}) collective-permute-start(f32[32,32]{0,1:T(8,128)S(1)} %add.162), channel_id=1, source_target_pairs={{0,2},{1,3},{2,0},{3,1},{4,6},{5,7},{6,4},{7,5},{8,10},{9,11},{10,... | collective-permute-start | bytes 12296 | tf_op jit(solution)/shard_map/ppermute | solution.py:30
  167.2 8.3 %collective-permute-start.11 = (f32[33,1536]{1,0:T(8,128)S(1)}, f32[33,1536]{1,0:T(8,128)S(1)}, u32[]{:S(2)}, u32[]{:S(2)}) collective-permute-start(f32[33,1536]{1,0:T(8,128)S(1)} %pad_maximum_fusion.7), channel_id=1, source_target_pairs={{0,1},{1,0},{2,3},{3,2},{4,5},{5,4},{6,7},{7,6},{8,9},{9,8},{10,11... | collective-permute-start | bytes 608264 | tf_op jit(solution)/shard_map/ppermute | solution.py:30
  175.4 36.2 %copy-start.4 = (f32[1,32,32]{1,2,0:T(8,128)}, f32[1,32,32]{1,2,0:T(8,128)S(1)}, u32[]{:S(2)}) copy-start(f32[1,32,32]{1,2,0:T(8,128)S(1)} %custom-call.22) | copy-start | bytes 12292
  176.4 11.0 %collective-permute-start.12 = (f32[33,1536]{1,0:T(8,128)S(1)}, f32[33,1536]{1,0:T(8,128)S(1)}, u32[]{:S(2)}, u32[]{:S(2)}) collective-permute-start(f32[33,1536]{1,0:T(8,128)S(1)} %fusion.53), channel_id=1, source_target_pairs={{0,2},{1,3},{2,0},{3,1},{4,6},{5,7},{6,4},{7,5},{8,10},{9,11},{10,... | collective-permute-start | bytes 608264 | tf_op jit(solution)/shard_map/ppermute | solution.py:30
  213.8 3.3 %copy-start.5 = (f32[1,32,32]{2,1,0:T(8,128)}, f32[1,32,32]{2,1,0:T(8,128)S(1)}, u32[]{:S(2)}) copy-start(f32[1,32,32]{2,1,0:T(8,128)S(1)} %convolution_bitcast_fusion) | copy-start | bytes 12292
  217.2 0.6 copy-start.6
  217.8 0.6 copy-start.2
  218.4 2.3 collective-permute-start.13
  222.9 9.8 %collective-permute-start.14 = (f32[33,2048]{1,0:T(8,128)S(1)}, f32[33,2048]{1,0:T(8,128)S(1)}, u32[]{:S(2)}, u32[]{:S(2)}) collective-permute-start(f32[33,2048]{1,0:T(8,128)S(1)} %pad_maximum_fusion.4), channel_id=1, source_target_pairs={{0,8},{4,12},{8,0},{12,4},{16,24},{20,28},{24,16},{28,20},{1,9},{5... | collective-permute-start | bytes 811016 | tf_op jit(solution)/shard_map/ppermute | solution.py:96
  232.8 9.0 %collective-permute-start.15 = (f32[33,2048]{1,0:T(8,128)S(1)}, f32[33,2048]{1,0:T(8,128)S(1)}, u32[]{:S(2)}, u32[]{:S(2)}) collective-permute-start(f32[33,2048]{1,0:T(8,128)S(1)} %pad_maximum_fusion.5), channel_id=1, source_target_pairs={{0,16},{4,20},{8,24},{12,28},{16,0},{20,4},{24,8},{28,12},{1,17},{... | collective-permute-start | bytes 811016 | tf_op jit(solution)/shard_map/ppermute | solution.py:103
  241.9 6.7 %collective-permute-start.18 = (f32[32,2048]{1,0:T(8,128)S(1)}, f32[32,2048]{1,0:T(8,128)S(1)}, u32[]{:S(2)}, u32[]{:S(2)}) collective-permute-start(f32[32,2048]{1,0:T(8,128)S(1)} %slice_add_fusion.2), channel_id=1, source_target_pairs={{0,8},{4,12},{8,0},{12,4},{16,24},{20,28},{24,16},{28,20},{1,9},{5... | collective-permute-start | bytes 786440 | tf_op jit(solution)/shard_map/ppermute | solution.py:109
  244.4 5.0 %collective-permute-start.16 = (f32[2,32,32]{2,1,0:T(8,128)S(1)}, f32[2,32,32]{2,1,0:T(8,128)S(1)}, u32[]{:S(2)}, u32[]{:S(2)}) collective-permute-start(f32[2,32,32]{2,1,0:T(8,128)S(1)} %add_add_fusion), channel_id=1, source_target_pairs={{0,1},{1,0},{2,3},{3,2},{4,5},{5,4},{6,7},{7,6},{8,9},{9,8},{10,11... | collective-permute-start | bytes 24584 | tf_op jit(solution)/shard_map/ppermute | solution.py:30
  248.6 7.2 %collective-permute-start.19 = (f32[32,4096]{1,0:T(8,128)S(1)}, f32[32,4096]{1,0:T(8,128)S(1)}, u32[]{:S(2)}, u32[]{:S(2)}) collective-permute-start(f32[32,4096]{1,0:T(8,128)S(1)} %maximum_select_fusion.4), channel_id=1, source_target_pairs={{0,4},{4,0},{8,12},{12,8},{16,20},{20,16},{24,28},{28,24},{1,5},{5... | collective-permute-start | bytes 1572872 | tf_op jit(solution)/shard_map/ppermute | solution.py:109
  249.5 5.2 %collective-permute-start.17 = (f32[2,32,32]{2,1,0:T(8,128)S(1)}, f32[2,32,32]{2,1,0:T(8,128)S(1)}, u32[]{:S(2)}, u32[]{:S(2)}) collective-permute-start(f32[2,32,32]{2,1,0:T(8,128)S(1)} %add.173), channel_id=1, source_target_pairs={{0,2},{1,3},{2,0},{3,1},{4,6},{5,7},{6,4},{7,5},{8,10},{9,11},{10,... | collective-permute-start | bytes 24584 | tf_op jit(solution)/shard_map/ppermute | solution.py:30
  258.7 3.8 %collective-permute-start.20 = (f32[32,32]{0,1:T(8,128)S(1)}, f32[32,32]{0,1:T(8,128)S(1)}, u32[]{:S(2)}, u32[]{:S(2)}) collective-permute-start(f32[32,32]{0,1:T(8,128)S(1)} %fusion.58), channel_id=1, source_target_pairs={{0,1},{1,0},{2,3},{3,2},{4,5},{5,4},{6,7},{7,6},{8,9},{9,8},{10,11... | collective-permute-start | bytes 12296 | tf_op jit(solution)/shard_map/ppermute | solution.py:30
  262.5 4.6 %collective-permute-start.21 = (f32[32,32]{0,1:T(8,128)S(1)}, f32[32,32]{0,1:T(8,128)S(1)}, u32[]{:S(2)}, u32[]{:S(2)}) collective-permute-start(f32[32,32]{0,1:T(8,128)S(1)} %add.176), channel_id=1, source_target_pairs={{0,2},{1,3},{2,0},{3,1},{4,6},{5,7},{6,4},{7,5},{8,10},{9,11},{10,... | collective-permute-start | bytes 12296 | tf_op jit(solution)/shard_map/ppermute | solution.py:30
